TPU v7x, 256 devices: a whole 4x4x8 slice. The times are simulated.
256 devices in a mesh: pipe: 8 (over z_hi, x), expert: 32 (over y, z_lo, core).
Axes of the slice: x: 4, y: 4, z: 8 (z_hi: 2, z_lo: 4; z = z_hi * 4 + z_lo), core: 2. Of those that a mesh axis runs over, the one named last changes fastest.
Arguments:
- grad_out: bfloat16 [8, 4096, 2048], P('pipe', 'expert'), may hold values from -6 to 6
- expert_ids: int32 [8, 4096, 8], P('pipe', 'expert'), may hold values from 0 to 63, as said below
- slot_ids: int32 [8, 4096, 8], P('pipe', 'expert'), may hold values from 0 to 16, as said below
- gate_weights: float32 [8, 4096, 8], P('pipe', 'expert'), may hold values from 0.02 to 0.6
- saved_pre: bfloat16 [8, 64, 512, 1536], P('pipe', 'expert'), may hold values from -6 to 6
- down_weight: bfloat16 [8, 64, 768, 2048], P('pipe', 'expert'), may hold values from -0.21875 to 0.21875
- router_weight: bfloat16 [8, 64, 2048], P('pipe', 'expert'), may hold values from -0.125 to 0.125
Outputs:
- pre_grad: bfloat16 [8, 64, 512, 1536], P('pipe', 'expert')
- grad_inputs: bfloat16 [8, 4096, 2048], P('pipe', 'expert')
Inputs may be any that keep to these rules, and one draw needn't show every extreme that they name: `expert_ids`: each row names 8 different experts. `slot_ids`: for the pair (t, k): the number of earlier pairs (by row, then by k) among the same device's 128 rows of that section that name the same expert, capped at 16; the value 16 marks a pair that is dropped.
All inputs are finite; a program needn't handle non-finite values.
Results may differ from a plain program's by a relative error of at most 0.012.
Values may be sent and summed in bfloat16 or wider, within the bound.
No kernel may reach another device: no remote copies, remote signals or barrier semaphores. Data moves between devices by JAX's collectives and lax.ppermute only.
A program may use at most 128 MiB of HBM per device.

v0:
```python
import jax
import jax.numpy as jnp
from jax import lax
from jax.sharding import PartitionSpec as P


def passed_along(value, axis, by):
    peers = lax.axis_size(axis)
    return lax.ppermute(value, axis, [(i, (i + by) % peers) for i in range(peers)])


def per_device(grad_out, expert_ids, slot_ids, gate_weights, saved_pre, down_weight, router_weight):
    groups = lax.axis_size("expert")
    local_experts = down_weight.shape[1]
    hidden_width = down_weight.shape[2]
    tok_rows = grad_out.shape[1]
    width = grad_out.shape[2]
    top_count = expert_ids.shape[2]
    expert_total = local_experts * groups
    capacity = tok_rows * top_count // expert_total
    total_rows = expert_total * capacity
    features = grad_out[0]
    next_features = passed_along(features, "pipe", -1)
    next_router = passed_along(router_weight[0], "pipe", -1)
    route_ids = expert_ids[0]
    kept_pairs = slot_ids[0] < capacity
    destination = (
        route_ids % local_experts * (groups * capacity)
        + route_ids // local_experts * capacity
        + jnp.minimum(slot_ids[0], capacity - 1)
    )
    pair_dest = jnp.where(kept_pairs, destination, total_rows)
    row_ids = jnp.arange(total_rows, dtype=jnp.int32)
    token_hit = pair_dest[None, :, :] == row_ids[:, None, None]
    token_onehot = jnp.any(token_hit, axis=2).astype(jnp.bfloat16)
    token_rows = jnp.dot(token_onehot, features, preferred_element_type=jnp.float32).astype(
        jnp.bfloat16
    )
    matches = token_hit.reshape(total_rows, tok_rows * top_count)
    gate_low = gate_weights[0].astype(jnp.bfloat16)
    slot_gate = jnp.sum(
        jnp.where(matches, gate_low.reshape(-1).astype(jnp.float32)[None, :], jnp.float32(0.0)),
        axis=1,
    )
    arrived = lax.all_to_all(
        token_rows.reshape(local_experts, groups, capacity, -1),
        "expert",
        split_axis=1,
        concat_axis=1,
        tiled=True,
    )
    me = lax.axis_index("expert")
    gate_table = (
        slot_gate.reshape(local_experts, groups, capacity)
        .transpose(1, 0, 2)
        .reshape(1, total_rows)
        .astype(jnp.bfloat16)
    )
    own_block = jnp.concatenate([gate_table, next_router.reshape(1, local_experts * width)], axis=1)
    blocks = lax.dynamic_update_slice(
        jnp.zeros((groups, own_block.shape[1]), jnp.bfloat16), own_block, (me, 0)
    )
    gathered = lax.psum(blocks, "expert")
    gate_in = (
        lax.dynamic_slice_in_dim(
            gathered[:, :total_rows],
            me * local_experts * capacity,
            local_experts * capacity,
            axis=1,
        )
        .reshape(groups, local_experts, capacity)
        .transpose(1, 0, 2)
        .reshape(local_experts, groups * capacity)
        .astype(jnp.float32)
    )
    next_router_full = gathered[:, total_rows:].reshape(expert_total, width)
    rows_in = arrived.reshape(local_experts, groups * capacity, -1).astype(jnp.float32)
    pre_saved = saved_pre[0]
    gate_part = pre_saved[..., :hidden_width].astype(jnp.float32)
    up_part = pre_saved[..., hidden_width:].astype(jnp.float32)
    sigmoid_gate = jax.nn.sigmoid(gate_part)
    silu_gate = gate_part * sigmoid_gate
    hidden = (silu_gate * up_part).astype(jnp.bfloat16)
    weights = down_weight[0]
    expert_out = jnp.einsum(
        "jsf,jfd->jsd", hidden, weights, preferred_element_type=jnp.float32
    ).astype(jnp.bfloat16)
    row_scores = jnp.sum(
        rows_in * lax.optimization_barrier(expert_out).astype(jnp.float32), axis=-1
    )
    returned = lax.all_to_all(
        row_scores.reshape(local_experts, groups, capacity),
        "expert",
        split_axis=1,
        concat_axis=1,
        tiled=True,
    )
    pair_scores = jnp.sum(
        jnp.where(matches, returned.reshape(total_rows)[:, None], jnp.float32(0.0)), axis=0
    ).reshape(tok_rows, top_count)
    scaled_rows = (gate_in[..., None] * rows_in).astype(jnp.bfloat16)
    row_grad = jnp.einsum("jsd,jfd->jsf", scaled_rows, weights, preferred_element_type=jnp.float32)
    gate_grad = row_grad * up_part * sigmoid_gate * (1.0 + gate_part * (1.0 - sigmoid_gate))
    up_grad = row_grad * silu_gate
    pre_grad = jnp.concatenate([gate_grad, up_grad], axis=-1).astype(jnp.bfloat16)
    gate_values = gate_weights[0]
    weighted_sum = jnp.sum(gate_values * pair_scores, axis=-1, keepdims=True)
    select_grad = gate_values * (pair_scores - weighted_sum)
    expert_columns = jnp.arange(expert_total, dtype=jnp.int32)
    chosen = route_ids[:, :, None] == expert_columns[None, None, :]
    logit_grad = jnp.sum(
        jnp.where(chosen, select_grad[:, :, None], jnp.float32(0.0)), axis=1
    ).astype(jnp.bfloat16)
    next_logit_grad = passed_along(logit_grad, "pipe", -1)
    router_part = jnp.dot(next_logit_grad, next_router_full, preferred_element_type=jnp.float32)
    outgoing = (next_features.astype(jnp.float32) + router_part).astype(jnp.bfloat16)
    return (pre_grad[None], outgoing[None])


def solution(mesh):
    in_specs = (
        P("pipe", "expert", None),
        P("pipe", "expert", None),
        P("pipe", "expert", None),
        P("pipe", "expert", None),
        P("pipe", "expert", None, None),
        P("pipe", "expert", None, None),
        P("pipe", "expert", None),
    )
    out_specs = (P("pipe", "expert", None, None), P("pipe", "expert", None))
    return jax.shard_map(
        per_device, mesh=mesh, in_specs=in_specs, out_specs=out_specs, check_vma=False
    )
```

profile of v0, /device:TPU:1, one launch (start us, length us, event | category | flops | bytes accessed | tf_op | source)
XLA Modules:
  0.0 472.0 jit_solution(9623698709281325380)
XLA Ops:
  7.2 0.7 fusion.27
  7.9 1.9 fusion.6
  9.8 2.3 convolution_convert_fusion
  12.1 2.3 copy.47
  14.4 0.0 copy-start.7
  14.4 0.0 copy-start.3
  14.4 10.4 %all-to-all-start = ((bf16[2,32,16,2048]{3,2,0,1:T(8,128)(2,1)}), bf16[2,32,16,2048]{3,2,0,1:T(8,128)(2,1)}, u32[]{:S(2)}, u32[]{:S(2)}) async-start(bf16[2,32,16,2048]{3,2,0,1:T(8,128)(2,1)} %copy.47), calls=%async_computation | async-start | bytes 8388608 | tf_op jit(solution)/shard_map/all_to_all | solution.py:45
  24.7 0.0 copy-done.7
  24.8 6.5 %collective-permute-start = (bf16[2,2048]{1,0:T(2,128)(2,1)S(1)}, bf16[2,2048]{1,0:T(2,128)(2,1)S(1)}, u32[]{:S(2)}, u32[]{:S(2)}) collective-permute-start(bf16[2,2048]{1,0:T(2,128)(2,1)S(1)} %bitcast.57), channel_id=1, source_target_pairs={{0,224},{32,0},{64,32},{96,64},{128,96},{160,128},{192,160},{224,1... | collective-permute-start | bytes 24584 | tf_op jit(solution)/shard_map/ppermute | solution.py:9
  31.2 0.0 copy-done.3
  31.2 0.5 collective-permute-start.1
  31.8 9.3 %fusion.7 = bf16[2,512,2048]{2,1,0:T(8,128)(2,1)} fusion(bf16[1,2,768,2048]{3,2,1,0:T(8,128)(2,1)} %param.12, bf16[2,512,1536]{2,1,0:T(8,128)(2,1)} %bitcast.55), kind=kOutput, calls=%fused_computation.18 | convolution fusion | flops 3229614080 | bytes 13631488 | tf_op jit(solution)/shard_map/jsf,jfd->jsd/dot_general | solution.py:85
  41.1 101.0 %all-to-all-done = bf16[2,32,16,2048]{3,2,0,1:T(8,128)(2,1)} async-done(((bf16[2,32,16,2048]{3,2,0,1:T(8,128)(2,1)}), bf16[2,32,16,2048]{3,2,0,1:T(8,128)(2,1)}, u32[]{:S(2)}, u32[]{:S(2)}) %all-to-all-start) | async-done | bytes 4194336 | tf_op jit(solution)/shard_map/all_to_all | solution.py:45
  142.1 0.0 copy-start.2
  142.1 3.4 copy.48
  145.5 0.0 copy-start
  145.5 3.2 copy-done
  148.7 0.0 copy-done.2
  148.7 0.0 copy-start.4
  148.7 0.9 fusion.1
  149.6 0.1 reshape.123
  149.7 0.6 copy.50
  150.3 4.7 all-to-all-start.1
  155.0 0.2 all-reduce.2.cloned.1.call-start
  155.2 0.0 copy-done.4
  155.3 0.1 copy.42
  155.4 0.1 copy.49
  155.5 0.1 eq.41
  155.6 0.1 copy.43
  155.7 0.1 reshape.126
  155.8 0.0 collective-permute-done
  155.8 6.8 %all-to-all-done.1 = f32[2,32,16]{2,0,1:T(2,128)S(1)} async-done(((f32[2,32,16]{2,0,1:T(2,128)}), f32[2,32,16]{2,0,1:T(2,128)S(1)}, u32[]{:S(2)}, u32[]{:S(2)}) %all-to-all-start.1) | async-done | bytes 4128 | tf_op jit(solution)/shard_map/all_to_all | solution.py:91
  162.6 0.1 broadcast_in_dim.58
  162.7 1.2 select_reduce_fusion
  163.8 0.1 convert_element_type.104
  164.0 0.1 convert_element_type.106
  164.1 0.6 copy.45
  164.7 0.2 broadcast_in_dim.54
  164.9 4.8 %dynamic_update_slice.3 = bf16[32,5120]{0,1:T(8,128)(2,1)S(1)} dynamic-update-slice(bf16[32,5120]{0,1:T(8,128)(2,1)S(1)} %broadcast_in_dim.54, bf16[1,5120]{0,1:T(8,128)(2,1)S(1)} %copy.45, s32[]{:T(128)S(6)} %select_n.41, s32[]{:T(128)} %constant.39.clone.1) | dynamic-update-slice | bytes 20484 | tf_op jit(solution)/shard_map/dynamic_update_slice | solution.py:60
  169.6 0.0 copy-start.1
  169.7 1.0 copy-done.1
  170.7 0.0 all-reduce.2.cloned.1.call-update
  170.7 0.1 reshape.124
  170.8 0.1 fusion.23
  170.9 0.1 bitcast_multiply_fusion.2
  171.1 0.0 copy-done.5
  171.1 0.1 select_reduce_fusion.2
  171.1 0.1 collective-permute-start.2
  171.2 276.7 %all-reduce.2.cloned.1.call-done = bf16[32,5120]{0,1:T(8,128)(2,1)} async-done(((bf16[32,5120]{0,1:T(8,128)(2,1)}), bf16[32,5120]{0,1:T(8,128)(2,1)}) %all-reduce.2.cloned.1.call-update) | async-done | bytes 327696 | tf_op jit(solution)/shard_map/psum | solution.py:63
  447.9 1.0 slice.16
  448.9 0.1 copy.46
  449.0 0.1 reshape.127
  449.1 0.0 copy-start.6
  449.1 4.0 fusion
  453.1 0.2 copy-done.6
  453.3 7.3 %fusion.20 = (bf16[1,2,512,768]{3,2,1,0:T(8,128)(2,1)S(1)}, bf16[1,2,512,768]{3,2,1,0:T(8,128)(2,1)S(1)}) fusion(bf16[2,512,1536]{2,1,0:T(8,128)(2,1)S(1)} %bitcast.56, bf16[2,512,2048]{2,1,0:T(8,128)(2,1)S(1)} %fusion, bf16[1,2,768,2048]{3,2,1,0:T(8,128)(2,1)} %param.12), kind=kOutput, calls=%fused_computation.31 | convolution fusion | flops 3233021952 | bytes 16777216 | tf_op jit(solution)/shard_map/jsd,jfd->jsf/dot_general | solution.py:102
  460.6 0.0 slice-start
  460.6 1.9 pad_maximum_fusion
  462.5 0.0 slice-done
  462.5 0.3 copy.53
  462.9 0.1 reshape.125
  463.0 0.0 collective-permute-done.1
  463.0 0.0 collective-permute-done.2
  463.0 2.2 fusion.22
  (9 shorter events, 0.1 us)
Async XLA Ops:
  14.4 10.4 %copy-start.7 = (bf16[1,2,2048]{2,1,0:T(2,128)(2,1)S(1)}, bf16[1,2,2048]{2,1,0:T(2,128)(2,1)}, u32[]{:S(2)}) copy-start(bf16[1,2,2048]{2,1,0:T(2,128)(2,1)} %param.13) | copy-start | bytes 24580
  14.4 16.9 %copy-start.3 = (bf16[1,128,2048]{2,1,0:T(8,128)(2,1)S(1)}, bf16[1,128,2048]{2,1,0:T(8,128)(2,1)}, u32[]{:S(2)}) copy-start(bf16[1,128,2048]{2,1,0:T(8,128)(2,1)} %param.7) | copy-start | bytes 1572868
  14.4 127.7 %all-to-all-start = ((bf16[2,32,16,2048]{3,2,0,1:T(8,128)(2,1)}), bf16[2,32,16,2048]{3,2,0,1:T(8,128)(2,1)}, u32[]{:S(2)}, u32[]{:S(2)}) async-start(bf16[2,32,16,2048]{3,2,0,1:T(8,128)(2,1)} %copy.47), calls=%async_computation | async-start | bytes 8388608 | tf_op jit(solution)/shard_map/all_to_all | solution.py:45
  24.8 131.0 %collective-permute-start = (bf16[2,2048]{1,0:T(2,128)(2,1)S(1)}, bf16[2,2048]{1,0:T(2,128)(2,1)S(1)}, u32[]{:S(2)}, u32[]{:S(2)}) collective-permute-start(bf16[2,2048]{1,0:T(2,128)(2,1)S(1)} %bitcast.57), channel_id=1, source_target_pairs={{0,224},{32,0},{64,32},{96,64},{128,96},{160,128},{192,160},{224,1... | collective-permute-start | bytes 24584 | tf_op jit(solution)/shard_map/ppermute | solution.py:9
  31.2 431.7 %collective-permute-start.1 = (bf16[128,2048]{1,0:T(8,128)(2,1)S(1)}, bf16[128,2048]{1,0:T(8,128)(2,1)}, u32[]{:S(2)}, u32[]{:S(2)}) collective-permute-start(bf16[128,2048]{1,0:T(8,128)(2,1)S(1)} %bitcast.48), channel_id=1, source_target_pairs={{0,224},{32,0},{64,32},{96,64},{128,96},{160,128},{192,160},{224,1... | collective-permute-start | bytes 1572872 | tf_op jit(solution)/shard_map/ppermute | solution.py:9
  142.1 6.6 %copy-start.2 = (bf16[2,512,2048]{2,1,0:T(8,128)(2,1)S(1)}, bf16[2,512,2048]{2,1,0:T(8,128)(2,1)}, u32[]{:S(2)}) copy-start(bf16[2,512,2048]{2,1,0:T(8,128)(2,1)} %fusion.7) | copy-start | bytes 12582916
  145.5 3.2 copy-start
  148.7 6.6 %copy-start.4 = (f32[1,128,8]{1,2,0:T(8,128)S(1)}, f32[1,128,8]{1,2,0:T(8,128)}, u32[]{:S(2)}) copy-start(f32[1,128,8]{1,2,0:T(8,128)} %param.10) | copy-start | bytes 12292
  150.3 12.3 %all-to-all-start.1 = ((f32[2,32,16]{2,0,1:T(2,128)}), f32[2,32,16]{2,0,1:T(2,128)S(1)}, u32[]{:S(2)}, u32[]{:S(2)}) async-start(f32[2,32,16]{2,0,1:T(2,128)} %copy.50), calls=%async_computation.1 | async-start | bytes 65536 | tf_op jit(solution)/shard_map/all_to_all | solution.py:91
  155.0 292.9 %all-reduce.2.cloned.1.call-start = ((), (), s32[]{:S(2)}) async-start(), calls=%async_computation.2 | async-start | bytes 2621440 | tf_op jit(solution)/shard_map/psum | solution.py:63
  164.7 6.4 %copy-start.5 = (s32[1,128,8]{1,2,0:T(8,128)S(1)}, s32[1,128,8]{1,2,0:T(8,128)}, u32[]{:S(2)}) copy-start(s32[1,128,8]{1,2,0:T(8,128)} %param.8) | copy-start | bytes 12292
  169.6 1.1 copy-start.1
  171.1 291.8 %collective-permute-start.2 = (bf16[128,64]{0,1:T(8,128)(2,1)S(1)}, bf16[128,64]{0,1:T(8,128)(2,1)S(1)}, u32[]{:S(2)}, u32[]{:S(2)}) collective-permute-start(bf16[128,64]{0,1:T(8,128)(2,1)S(1)} %select_reduce_fusion.2), channel_id=1, source_target_pairs={{0,224},{32,0},{64,32},{96,64},{128,96},{160,128},{192,160},{224,1... | collective-permute-start | bytes 49160 | tf_op jit(solution)/shard_map/ppermute | solution.py:9
  449.1 4.3 copy-start.6
  460.6 1.9 slice-start
Sparse Core Ops, SparseCore 0:
  170.8 276.9 all-reduce.1
where the time goes:
time: 472 us
  waiting for transfers between devices  384 us (81%)
  starting transfers between devices  22.4 us (5%)
  matrix products  21 us (4%)
  local copies, waits for them, and re-layouts  18.9 us (4%)
  between operations  14.3 us (3%)
  other arithmetic  10.9 us (2%)
    psum x1, waiting for transfers between devices, per_device(): gathered = lax.psum(blocks, 'expert')  277 us
    all_to_all x1, waiting for transfers between devices, per_device(): lax.all_to_all(token_rows.reshape(local_experts, groups, capacity, -1), '...  101 us
    all_to_all x1, starting transfers between devices, per_device(): lax.all_to_all(token_rows.reshape(local_experts, groups, capacity, -1), '...  10.4 us
  transfers between devices with their start and end apart: 6, of which 3 were waited for; matrix products, arithmetic and copies ran while one was open for 8% of the time, Pallas kernels for 0%

commit v1 on v0

--- a/solution.py
+++ b/solution.py
@@ -60,7 +60,7 @@
     blocks = lax.dynamic_update_slice(
         jnp.zeros((groups, own_block.shape[1]), jnp.bfloat16), own_block, (me, 0)
     )
-    gathered = lax.psum(blocks, "expert")
+    gathered = jnp.sum(lax.all_gather(blocks, "expert"), axis=0)
     gate_in = (
         lax.dynamic_slice_in_dim(
             gathered[:, :total_rows],

time: 472 us -> 258 us (0.55)
  waiting for transfers between devices: 384 us -> 165 us
  local copies, waits for them, and re-layouts: 18.9 us -> 12.3 us
  other arithmetic: 10.9 us -> 17.3 us
  starting transfers between devices: 22.4 us -> 28.5 us
    psum x1 -> x0, waiting for transfers between devices: 277 us -> none  [per_device(): gathered = lax.psum(blocks, 'expert')]
    all_gather x0 -> x1, waiting for transfers between devices: none -> 79.3 us  [per_device(): gathered = jnp.sum(lax.all_gather(blocks, 'expert'), axis=0)]
    all_to_all x1, waiting for transfers between devices: 101 us -> 79.1 us  [per_device(): lax.all_to_all(token_rows.reshape(local_experts, groups, capacity, -1), '...]
    ppermute x3, starting transfers between devices: 7.11 us -> 13.4 us  [passed_along(): lax.ppermute(value, axis, [(i, (i + by) % peers) for i in range(peers)])]
    reduce_sum x0 -> x1, other arithmetic: none -> 6.24 us  [per_device(): gathered = jnp.sum(lax.all_gather(blocks, 'expert'), axis=0)]
  transfers between devices with their start and end apart: 6 -> 6, of which waited for: 3 -> 3; matrix products, arithmetic and copies ran while one was open for 8% -> 14% of each run, Pallas kernels for 0% -> 0%
where the time goes in v1:
time: 258 us
  waiting for transfers between devices  165 us (64%)
  starting transfers between devices  28.5 us (11%)
  matrix products  20 us (8%)
  other arithmetic  17.3 us (7%)
  between operations  14.3 us (6%)
  local copies, waits for them, and re-layouts  12.3 us (5%)
    all_gather x1, waiting for transfers between devices, per_device(): gathered = jnp.sum(lax.all_gather(blocks, 'expert'), axis=0)  79.3 us
    all_to_all x1, waiting for transfers between devices, per_device(): lax.all_to_all(token_rows.reshape(local_experts, groups, capacity, -1), '...  79.1 us
    ppermute x3, starting transfers between devices, passed_along(): lax.ppermute(value, axis, [(i, (i + by) % peers) for i in range(peers)])  13.4 us
    all_to_all x1, starting transfers between devices, per_device(): lax.all_to_all(token_rows.reshape(local_experts, groups, capacity, -1), '...  10.4 us
    dot_general x1, matrix products, per_device(): jnp.einsum('jsf,jfd->jsd', hidden, weights, preferred_element_type=jnp.fl...  9.29 us
    dot_general x1, matrix products, per_device(): jnp.einsum('jsd,jfd->jsf', scaled_rows, weights, preferred_element_type=j...  7.27 us
    all_to_all x1, waiting for transfers between devices, per_device(): lax.all_to_all(row_scores.reshape(local_experts, groups, capacity), 'expe...  7.06 us
    reduce_sum x1, other arithmetic, per_device(): gathered = jnp.sum(lax.all_gather(blocks, 'expert'), axis=0)  6.24 us
  transfers between devices with their start and end apart: 6, of which 3 were waited for; matrix products, arithmetic and copies ran while one was open for 14% of the time, Pallas kernels for 0%

profile of v1, /device:TPU:1, one launch (start us, length us, event | category | flops | bytes accessed | tf_op | source)
XLA Modules:
  0.0 257.7 jit_solution(5954739009737398312)
XLA Ops:
  7.2 0.7 fusion.27
  7.9 1.9 fusion.6
  9.8 2.3 convolution_convert_fusion
  12.1 2.3 copy.56
  14.4 0.0 copy-start.7
  14.4 10.4 %all-to-all-start = ((bf16[2,32,16,2048]{3,2,0,1:T(8,128)(2,1)}), bf16[2,32,16,2048]{3,2,0,1:T(8,128)(2,1)}, u32[]{:S(2)}, u32[]{:S(2)}) async-start(bf16[2,32,16,2048]{3,2,0,1:T(8,128)(2,1)} %copy.56), calls=%async_computation | async-start | bytes 8388608 | tf_op jit(solution)/shard_map/all_to_all | solution.py:45
  24.8 0.0 copy-done.7
  24.8 6.5 %collective-permute-start = (bf16[2,2048]{1,0:T(2,128)(2,1)S(1)}, bf16[2,2048]{1,0:T(2,128)(2,1)S(1)}, u32[]{:S(2)}, u32[]{:S(2)}) collective-permute-start(bf16[2,2048]{1,0:T(2,128)(2,1)S(1)} %bitcast.58), channel_id=1, source_target_pairs={{0,224},{32,0},{64,32},{96,64},{128,96},{160,128},{192,160},{224,1... | collective-permute-start | bytes 24584 | tf_op jit(solution)/shard_map/ppermute | solution.py:9
  31.3 9.3 %fusion.7 = bf16[2,512,2048]{2,1,0:T(8,128)(2,1)} fusion(bf16[1,2,768,2048]{3,2,1,0:T(8,128)(2,1)} %param.12, bf16[2,512,1536]{2,1,0:T(8,128)(2,1)} %bitcast.56), kind=kOutput, calls=%fused_computation.18 | convolution fusion | flops 3229614080 | bytes 13631488 | tf_op jit(solution)/shard_map/jsf,jfd->jsd/dot_general | solution.py:85
  40.6 79.1 %all-to-all-done = bf16[2,32,16,2048]{3,2,0,1:T(8,128)(2,1)} async-done(((bf16[2,32,16,2048]{3,2,0,1:T(8,128)(2,1)}), bf16[2,32,16,2048]{3,2,0,1:T(8,128)(2,1)}, u32[]{:S(2)}, u32[]{:S(2)}) %all-to-all-start) | async-done | bytes 4194336 | tf_op jit(solution)/shard_map/all_to_all | solution.py:45
  119.6 0.0 copy-start.1
  119.6 3.4 %copy.57 = f32[2,32,16,2048]{3,2,1,0:T(8,128)S(1)} copy(bf16[2,32,16,2048]{3,2,0,1:T(8,128)(2,1)} %all-to-all-done) | data formatting | bytes 12582912 | tf_op jit(solution)/shard_map/convert_element_type | solution.py:77
  123.0 0.0 copy-start
  123.0 3.3 %copy-done = f32[2,32,16,2048]{3,2,1,0:T(8,128)} copy-done((f32[2,32,16,2048]{3,2,1,0:T(8,128)}, f32[2,32,16,2048]{3,2,1,0:T(8,128)S(1)}, u32[]{:S(2)}) %copy-start) | copy-done | bytes 8388632
  126.4 0.0 copy-done.1
  126.4 0.0 copy-start.4
  126.4 0.0 copy-start.3
  126.4 0.0 copy-start.5
  126.4 0.9 fusion.1
  127.3 0.1 reshape.125
  127.4 0.6 copy.59
  128.0 4.7 %all-to-all-start.1 = ((f32[2,32,16]{2,0,1:T(2,128)}), f32[2,32,16]{2,0,1:T(2,128)S(1)}, u32[]{:S(2)}, u32[]{:S(2)}) async-start(f32[2,32,16]{2,0,1:T(2,128)} %copy.59), calls=%async_computation.1 | async-start | bytes 65536 | tf_op jit(solution)/shard_map/all_to_all | solution.py:91
  132.7 0.0 all-gather.2.cloned.1.call-start
  132.8 0.0 copy-done.4
  132.8 0.1 copy.51
  132.9 0.1 eq.41
  133.0 0.1 copy.52
  133.1 0.1 reshape.128
  133.2 0.0 collective-permute-done
  133.2 7.1 %all-to-all-done.1 = f32[2,32,16]{2,0,1:T(2,128)S(1)} async-done(((f32[2,32,16]{2,0,1:T(2,128)}), f32[2,32,16]{2,0,1:T(2,128)S(1)}, u32[]{:S(2)}, u32[]{:S(2)}) %all-to-all-start.1) | async-done | bytes 4128 | tf_op jit(solution)/shard_map/all_to_all | solution.py:91
  140.3 0.1 broadcast_in_dim.58
  140.3 1.2 select_reduce_fusion
  141.5 0.1 convert_element_type.106
  141.7 0.1 convert_element_type.108
  141.8 0.3 dynamic_update_slice.4
  142.1 0.0 copy-start.2
  142.1 0.7 copy-done.2
  142.8 0.0 all-gather.2.cloned.1.call-update
  142.9 0.0 copy-done.3
  142.9 6.3 %collective-permute-start.1 = (bf16[128,2048]{1,0:T(8,128)(2,1)S(1)}, bf16[128,2048]{1,0:T(8,128)(2,1)S(1)}, u32[]{:S(2)}, u32[]{:S(2)}) collective-permute-start(bf16[128,2048]{1,0:T(8,128)(2,1)S(1)} %bitcast.49), channel_id=1, source_target_pairs={{0,224},{32,0},{64,32},{96,64},{128,96},{160,128},{192,160},{224,1... | collective-permute-start | bytes 1572872 | tf_op jit(solution)/shard_map/ppermute | solution.py:9
  149.1 0.1 copy.58
  149.2 0.1 reshape.126
  149.3 0.1 fusion.23
  149.4 0.1 bitcast_multiply_fusion.2
  149.6 0.0 copy-done.5
  149.6 0.1 select_reduce_fusion.2
  149.7 0.6 collective-permute-start.2
  150.3 79.3 %all-gather.2.cloned.1.call-done = bf16[32,32,5120]{2,1,0:T(8,128)(2,1)} async-done(((bf16[1,32,5120]{2,1,0:T(8,128)(2,1)}), bf16[32,32,5120]{2,1,0:T(8,128)(2,1)}) %all-gather.2.cloned.1.call-update) | async-done | bytes 10485776 | tf_op jit(solution)/shard_map/all_gather | solution.py:63
  229.6 6.2 %reduce_sum.58 = bf16[32,5120]{1,0:T(8,128)(2,1)S(1)} reduce(bf16[32,32,5120]{2,1,0:T(8,128)(2,1)} %all-gather.2.cloned.1.call-done, bf16[]{:T(256)} %constant.39.clone.1), dimensions={0}, to_apply=%region_1.2 | reduce | flops 5079040 | bytes 10813442 | tf_op jit(solution)/shard_map/reduce_sum | solution.py:63
  235.8 0.1 dynamic-slice_convert_fusion
  235.9 0.1 copy.54
  236.0 0.1 copy.55
  236.1 0.1 reshape.129
  236.2 0.0 copy-start.6
  236.2 4.0 %fusion = bf16[2,512,2048]{2,1,0:T(8,128)(2,1)S(1)} fusion(f32[2,32,16,2048]{3,2,1,0:T(8,128)} %copy-done, f32[2,512]{1,0:T(2,128)S(1)} %reshape.129), kind=kLoop, calls=%fused_computation.2 | loop fusion | flops 4194304 | bytes 12587008 | tf_op jit(solution)/shard_map/convert_element_type | solution.py:101
  240.2 0.2 copy-done.6
  240.4 7.3 %fusion.20 = (bf16[1,2,512,768]{3,2,1,0:T(8,128)(2,1)S(1)}, bf16[1,2,512,768]{3,2,1,0:T(8,128)(2,1)S(1)}) fusion(bf16[2,512,1536]{2,1,0:T(8,128)(2,1)S(1)} %bitcast.57, bf16[2,512,2048]{2,1,0:T(8,128)(2,1)S(1)} %fusion, bf16[1,2,768,2048]{3,2,1,0:T(8,128)(2,1)} %param.12), kind=kOutput, calls=%fused_computation.31 | convolution fusion | flops 3233021952 | bytes 16777216 | tf_op jit(solution)/shard_map/jsd,jfd->jsf/dot_general | solution.py:102
  247.7 1.9 pad_maximum_fusion
  249.7 0.1 reshape.127
  249.8 0.0 collective-permute-done.1
  249.8 0.0 collective-permute-done.2
  249.8 1.1 fusion.22
  (9 shorter events, 0.2 us)
Async XLA Ops:
  14.4 10.4 %copy-start.7 = (bf16[1,2,2048]{2,1,0:T(2,128)(2,1)S(1)}, bf16[1,2,2048]{2,1,0:T(2,128)(2,1)}, u32[]{:S(2)}) copy-start(bf16[1,2,2048]{2,1,0:T(2,128)(2,1)} %param.13) | copy-start | bytes 24580
  14.4 105.2 %all-to-all-start = ((bf16[2,32,16,2048]{3,2,0,1:T(8,128)(2,1)}), bf16[2,32,16,2048]{3,2,0,1:T(8,128)(2,1)}, u32[]{:S(2)}, u32[]{:S(2)}) async-start(bf16[2,32,16,2048]{3,2,0,1:T(8,128)(2,1)} %copy.56), calls=%async_computation | async-start | bytes 8388608 | tf_op jit(solution)/shard_map/all_to_all | solution.py:45
  24.8 108.4 %collective-permute-start = (bf16[2,2048]{1,0:T(2,128)(2,1)S(1)}, bf16[2,2048]{1,0:T(2,128)(2,1)S(1)}, u32[]{:S(2)}, u32[]{:S(2)}) collective-permute-start(bf16[2,2048]{1,0:T(2,128)(2,1)S(1)} %bitcast.58), channel_id=1, source_target_pairs={{0,224},{32,0},{64,32},{96,64},{128,96},{160,128},{192,160},{224,1... | collective-permute-start | bytes 24584 | tf_op jit(solution)/shard_map/ppermute | solution.py:9
  119.6 6.7 %copy-start.1 = (bf16[2,512,2048]{2,1,0:T(8,128)(2,1)S(1)}, bf16[2,512,2048]{2,1,0:T(8,128)(2,1)}, u32[]{:S(2)}) copy-start(bf16[2,512,2048]{2,1,0:T(8,128)(2,1)} %fusion.7) | copy-start | bytes 12582916
  123.0 3.3 %copy-start = (f32[2,32,16,2048]{3,2,1,0:T(8,128)}, f32[2,32,16,2048]{3,2,1,0:T(8,128)S(1)}, u32[]{:S(2)}) copy-start(f32[2,32,16,2048]{3,2,1,0:T(8,128)S(1)} %copy.57) | copy-start | bytes 25165828
  126.4 6.4 %copy-start.4 = (f32[1,128,8]{1,2,0:T(8,128)S(1)}, f32[1,128,8]{1,2,0:T(8,128)}, u32[]{:S(2)}) copy-start(f32[1,128,8]{1,2,0:T(8,128)} %param.10) | copy-start | bytes 12292
  126.4 16.5 %copy-start.3 = (bf16[1,128,2048]{2,1,0:T(8,128)(2,1)S(1)}, bf16[1,128,2048]{2,1,0:T(8,128)(2,1)}, u32[]{:S(2)}) copy-start(bf16[1,128,2048]{2,1,0:T(8,128)(2,1)} %param.7) | copy-start | bytes 1572868
  126.4 23.2 %copy-start.5 = (s32[1,128,8]{1,2,0:T(8,128)S(1)}, s32[1,128,8]{1,2,0:T(8,128)}, u32[]{:S(2)}) copy-start(s32[1,128,8]{1,2,0:T(8,128)} %param.8) | copy-start | bytes 12292
  128.0 12.3 %all-to-all-start.1 = ((f32[2,32,16]{2,0,1:T(2,128)}), f32[2,32,16]{2,0,1:T(2,128)S(1)}, u32[]{:S(2)}, u32[]{:S(2)}) async-start(f32[2,32,16]{2,0,1:T(2,128)} %copy.59), calls=%async_computation.1 | async-start | bytes 65536 | tf_op jit(solution)/shard_map/all_to_all | solution.py:91
  132.7 96.9 %all-gather.2.cloned.1.call-start = ((), (), s32[]{:S(2)}) async-start(), calls=%async_computation.2 | async-start | bytes 10813440 | tf_op jit(solution)/shard_map/all_gather | solution.py:63
  142.1 0.7 copy-start.2
  142.9 106.9 %collective-permute-start.1 = (bf16[128,2048]{1,0:T(8,128)(2,1)S(1)}, bf16[128,2048]{1,0:T(8,128)(2,1)S(1)}, u32[]{:S(2)}, u32[]{:S(2)}) collective-permute-start(bf16[128,2048]{1,0:T(8,128)(2,1)S(1)} %bitcast.49), channel_id=1, source_target_pairs={{0,224},{32,0},{64,32},{96,64},{128,96},{160,128},{192,160},{224,1... | collective-permute-start | bytes 1572872 | tf_op jit(solution)/shard_map/ppermute | solution.py:9
  149.7 100.1 %collective-permute-start.2 = (bf16[128,64]{0,1:T(8,128)(2,1)S(1)}, bf16[128,64]{0,1:T(8,128)(2,1)S(1)}, u32[]{:S(2)}, u32[]{:S(2)}) collective-permute-start(bf16[128,64]{0,1:T(8,128)(2,1)S(1)} %select_reduce_fusion.2), channel_id=1, source_target_pairs={{0,224},{32,0},{64,32},{96,64},{128,96},{160,128},{192,160},{224,1... | collective-permute-start | bytes 49160 | tf_op jit(solution)/shard_map/ppermute | solution.py:9
  236.2 4.3 %copy-start.6 = (bf16[1,2,512,1536]{3,2,1,0:T(8,128)(2,1)S(1)}, bf16[1,2,512,1536]{3,2,1,0:T(8,128)(2,1)}, u32[]{:S(2)}) copy-start(bf16[1,2,512,1536]{3,2,1,0:T(8,128)(2,1)} %param.11) | copy-start | bytes 9437188
Sparse Core Ops, SparseCore 0:
  143.0 86.5 all-gather.1
